TPU v7x, 32 devices: a whole 2x2x4 slice. The times are simulated.
32 devices in a mesh: req: 8 (over y, x, core), head: 4 (over z).
Axes of the slice: x: 2, y: 2, z: 4, core: 2. Of those that a mesh axis runs over, the one named last changes fastest.
Arguments:
- queries: bfloat16 [4096, 8192], P('req', 'head'), may hold values from -150 to 150, as said below
- new_keys: bfloat16 [4096, 1024], P('req', 'head'), may hold values from -6 to 6, as said below
- fresh_values: bfloat16 [4096, 1024], P('req', 'head'), may hold values from -6 to 6
- key_page_pool: bfloat16 [224, 128, 1024], P('req', None, 'head'), may hold values from -6 to 6
- value_page_pool: bfloat16 [224, 128, 1024], P('req', None, 'head'), may hold values from -6 to 6
- page_table: int32 [16, 14], P('req'), may hold values from 0 to 27, as said below
- new_counts: int32 [16], P('req'), may hold values from 1 to 256, 2048 in all
- cached_lens: int32 [16], P('req'), may hold values from 1 to 1536, 8192 in all
- deal_offset: int32 [8], P('req'), may hold values from 0 to 7
- residual: bfloat16 [2112, 8192], P('req', 'head'), may hold values from -1.1953125 to 1.1953125
- out_weight: bfloat16 [8192, 8192], P('head', 'req'), may hold values from -0.09375 to 0.09375
Outputs:
- hidden: bfloat16 [2112, 8192], P('req', 'head')
- keys_out: bfloat16 [224, 128, 1024], P('req', None, 'head')
- values_out: bfloat16 [224, 128, 1024], P('req', None, 'head')
Inputs may be any that keep to these rules, and one draw needn't show every extreme that they name: `new_counts`: the counts sum to 2048; the largest is exactly 256. `cached_lens`: the counts sum to 8192; the largest is exactly 1536. `page_table`: the 2 rows of each aligned block of requests hold together each of 0 to 27 once. `queries`: real values. `new_keys`: real values.
All inputs are finite; a program needn't handle non-finite values. No bound on the sum of `new_counts` or of `cached_lens` on one device may be relied on, other than what follows from the above.
Results may differ from a plain program's by a relative error of at most 0.0085.
Values may be sent and summed in bfloat16 or wider, within the bound.
No kernel may reach another device: no remote copies, remote signals or barrier semaphores. Data moves between devices by JAX's collectives and lax.ppermute only.
A program may use at most 128 MiB of HBM per device.

v0:
```python
import math
import jax
import jax.numpy as jnp
from jax import lax
from jax.sharding import PartitionSpec as P

HEAD_SIZE = 128
NEGATIVE = -1e30


def head_attention(query_matrix, prior_keys, prior_values, visible, scale_factor):
    scores = (
        jnp.einsum("tkd,skd->kts", query_matrix, prior_keys, preferred_element_type=jnp.float32)
        * scale_factor
    )
    spots_all = jnp.arange(prior_keys.shape[0], dtype=jnp.int32)
    allowed = spots_all[None, None, :] <= visible[None, :, None]
    scores = jnp.where(allowed, scores, NEGATIVE)
    highest = jnp.max(scores, axis=2, keepdims=True)
    expo_terms = jnp.where(allowed, jnp.exp(scores - highest), 0.0)
    weights = (expo_terms / jnp.sum(expo_terms, axis=2, keepdims=True)).astype(jnp.bfloat16)
    mixed = jnp.einsum("kts,skd->tkd", weights, prior_values, preferred_element_type=jnp.float32)
    return mixed.astype(jnp.bfloat16)


def deal(row_block, new_counts, lead_in, shares, starts, totals, balanced):
    groups = lax.axis_size("req")
    my_rank = lax.axis_index("req")
    per_group = new_counts.shape[0]
    new_limit = row_block.shape[0] // per_group
    pair_slots = row_block.shape[0] // groups
    columns = row_block.shape[1]
    own_lead = lax.dynamic_index_in_dim(lead_in, my_rank, 0, keepdims=False)
    ordinal = jnp.arange(pair_slots, dtype=jnp.int32)[None, :] * groups + own_lead[:, None]
    ends_at = jnp.cumsum(new_counts)
    request_index = jnp.sum(
        (ordinal[:, :, None] >= ends_at[None, None, :]).astype(jnp.int32), axis=2
    )
    request_index = jnp.minimum(request_index, per_group - 1)
    before = ends_at - new_counts
    source = request_index * new_limit + ordinal - jnp.take(before, request_index)
    own_total = lax.dynamic_index_in_dim(totals, my_rank, 0, keepdims=False)
    is_live = ordinal < own_total
    source = jnp.where(is_live, source, 0)
    picked = jnp.take(row_block, source.reshape(-1), axis=0).reshape(groups, pair_slots, columns)
    outgoing = jnp.where(is_live[:, :, None], picked, jnp.zeros((), row_block.dtype))
    arrived = lax.all_to_all(outgoing, "req", split_axis=0, concat_axis=0, tiled=True)
    own_shares = lax.dynamic_index_in_dim(shares, my_rank, 1, keepdims=False)
    own_starts = lax.dynamic_index_in_dim(starts, my_rank, 1, keepdims=False)
    within = jnp.arange(pair_slots, dtype=jnp.int32)[None, :]
    landing = jnp.where(within < own_shares[:, None], own_starts[:, None] + within, balanced)
    blank_rows = jnp.zeros((balanced, columns), row_block.dtype)
    return blank_rows.at[landing.reshape(-1)].set(arrived.reshape(-1, columns), mode="drop")


def project(row_block, out_weight):
    return jnp.dot(
        row_block,
        lax.all_gather(out_weight, "req", axis=1, tiled=True),
        preferred_element_type=jnp.float32,
    )


def head_total(partial_sum):
    return lax.psum_scatter(
        partial_sum.astype(jnp.bfloat16), "head", scatter_dimension=1, tiled=True
    ).astype(jnp.float32)


def local(
    queries,
    new_keys,
    fresh_values,
    key_page_pool,
    value_page_pool,
    page_table,
    new_counts,
    cached_lens,
    deal_offset,
    residual,
    out_weight,
):
    groups = lax.axis_size("req")
    per_group = new_counts.shape[0]
    page_count = page_table.shape[1]
    page_rows = key_page_pool.shape[1]
    channel_count = key_page_pool.shape[2]
    kv_local = channel_count // HEAD_SIZE
    slot_count = queries.shape[0]
    new_limit = slot_count // per_group
    q_width = queries.shape[1]
    group_fanout = q_width // channel_count
    balanced = residual.shape[0]
    new_slot = jnp.arange(new_limit, dtype=jnp.int32)
    positions = cached_lens[:, None] + new_slot[None, :]
    page_of = jnp.take_along_axis(page_table, positions // page_rows, axis=1)
    outside = key_page_pool.shape[0] * page_rows
    target = jnp.where(
        new_slot[None, :] < new_counts[:, None],
        page_of * page_rows + positions % page_rows,
        outside,
    ).reshape(-1)
    flat_keys = key_page_pool.reshape(-1, channel_count).at[target].set(new_keys, mode="drop")
    flat_values = (
        value_page_pool.reshape(-1, channel_count).at[target].set(fresh_values, mode="drop")
    )
    gathered_keys = flat_keys.reshape(key_page_pool.shape)
    gathered_values = flat_values.reshape(value_page_pool.shape)
    scale_factor = 1.0 / math.sqrt(HEAD_SIZE)
    pieces = []
    for member in range(per_group):
        prior_keys = gathered_keys[page_table[member]].reshape(
            page_count * page_rows, kv_local, HEAD_SIZE
        )
        prior_values = gathered_values[page_table[member]].reshape(
            page_count * page_rows, kv_local, HEAD_SIZE
        )
        query_matrix = queries[member * new_limit : (member + 1) * new_limit].reshape(
            new_limit, kv_local, group_fanout, HEAD_SIZE
        )
        query_matrix = jnp.moveaxis(query_matrix, 2, 0)
        visible = positions[member]
        mixed = lax.map(
            lambda single: head_attention(single, prior_keys, prior_values, visible, scale_factor),
            query_matrix,
        )
        pieces.append(jnp.moveaxis(mixed, 0, 2).reshape(new_limit, q_width))
    attended = jnp.concatenate(pieces, axis=0)
    load_counts, offsets_all = (
        lax.all_gather(new_counts, "req", axis=0, tiled=True),
        lax.all_gather(deal_offset, "req", axis=0, tiled=True),
    )
    totals = jnp.sum(load_counts.reshape(groups, per_group), axis=1)
    rank_ids = jnp.arange(groups, dtype=jnp.int32)
    lead_in = jnp.remainder(rank_ids[None, :] - offsets_all[:, None], groups)
    shares = jnp.maximum((totals[:, None] - lead_in + groups - 1) // groups, 0)
    starts = jnp.cumsum(shares, axis=0) - shares
    summed = head_total(project(attended, out_weight)).astype(jnp.bfloat16)
    placed = deal(summed, new_counts, lead_in, shares, starts, totals, balanced)
    hidden = (residual.astype(jnp.float32) + placed.astype(jnp.float32)).astype(jnp.bfloat16)
    return (hidden, gathered_keys, gathered_values)


def solution(mesh):
    placed = (
        P("req", "head"),
        P("req", "head"),
        P("req", "head"),
        P("req", None, "head"),
        P("req", None, "head"),
        P("req", None),
        P("req"),
        P("req"),
        P("req"),
        P("req", "head"),
        P("head", "req"),
    )
    return jax.shard_map(
        local,
        mesh=mesh,
        in_specs=placed,
        out_specs=(P("req", "head"), P("req", None, "head"), P("req", None, "head")),
        check_vma=False,
    )
```

profile of v0, /device:TPU:0, one launch (start us, length us, event | category | flops | bytes accessed | tf_op | source)
XLA Modules:
  0.0 404.9 jit_solution(16835856660951470666)
XLA Ops:
  11.1 4.7 %gather_fusion.6 = s32[512]{0:T(512)S(1)} fusion(s32[2,14]{1,0:T(2,128)S(1)} %copy-done, s32[512]{0:T(512)S(1)} %bitcast.125), kind=kCustom, calls=%fused_computation.6 | custom fusion | bytes 8192 | tf_op jit(solution)/shard_map/jit(take_along_axis)/gather | solution.py:96
  15.9 5.5 %scatter_fusion = bf16[3584,256]{1,0:T(8,128)(2,1)} fusion(bf16[3584,256]{1,0:T(8,128)(2,1)} %bitcast.130, s32[512]{0:T(512)S(1)} %bitcast.143, bf16[512,256]{1,0:T(8,128)(2,1)S(1)} %copy-done.7), kind=kCustom, calls=%fused_computation.7 | custom fusion | bytes 788480 | tf_op jit(solution)/shard_map/scatter | solution.py:103
  48.2 66.8 %while.21 = (s32[]{:T(128)}, bf16[8,256,2,128]{1,3,0,2:T(8,128)(2,1)S(1)}, s32[1,256]{1,0:T(1,128)S(1)}, bf16[8,256,2,128]{1,3,0,2:T(8,128)(2,1)}, bf16[1792,2,1...) while((s32[]{:T(128)}, bf16[8,256,2,128]{1,3,0,2:T(8,128)(2,1)S(1)}, ...), condition=%wide.region_13.14_spmd, body=%wide.region_10.13_spmd.sunk | while | flops 476710656 | bytes 11342941 | solution.py:123
  48.5 4.6 %fusion.93 = (f32[2,256]{1,0:T(2,128)S(1)}, f32[2,256,1792]{2,1,0:T(8,128)}) fusion(bf16[1792,2,128]{2,0,1:T(8,128)(2,1)S(1)} %get-tuple-element.251, pred[256,1792]{1,0:T(8,128)(4,1)S(1)} %iota_compare_fusion.6, bf16[8,256,2,128]{1,3,0,2:T(8,128)(2,1)} %get-tuple-element.250, s32[]{:T(128)S(6)} %copy.63), kind=kOutput, calls=%fused_computation.132.clone.1 | convolution fusion | flops 239470336 | bytes 5638148 | tf_op jit(solution)/shard_map/while/body/eval_jaxpr/sub | solution.py:20
  56.6 4.6 %fusion.93 = (f32[2,256]{1,0:T(2,128)S(1)}, f32[2,256,1792]{2,1,0:T(8,128)}) fusion(bf16[1792,2,128]{2,0,1:T(8,128)(2,1)S(1)} %get-tuple-element.251, pred[256,1792]{1,0:T(8,128)(4,1)S(1)} %iota_compare_fusion.6, bf16[8,256,2,128]{1,3,0,2:T(8,128)(2,1)} %get-tuple-element.250, s32[]{:T(128)S(6)} %copy.63), kind=kOutput, calls=%fused_computation.132.clone.1 | convolution fusion | flops 239470336 | bytes 5638148 | tf_op jit(solution)/shard_map/while/body/eval_jaxpr/sub | solution.py:20
  64.7 4.6 %fusion.93 = (f32[2,256]{1,0:T(2,128)S(1)}, f32[2,256,1792]{2,1,0:T(8,128)}) fusion(bf16[1792,2,128]{2,0,1:T(8,128)(2,1)S(1)} %get-tuple-element.251, pred[256,1792]{1,0:T(8,128)(4,1)S(1)} %iota_compare_fusion.6, bf16[8,256,2,128]{1,3,0,2:T(8,128)(2,1)} %get-tuple-element.250, s32[]{:T(128)S(6)} %copy.63), kind=kOutput, calls=%fused_computation.132.clone.1 | convolution fusion | flops 239470336 | bytes 5638148 | tf_op jit(solution)/shard_map/while/body/eval_jaxpr/sub | solution.py:20
  72.8 4.6 %fusion.93 = (f32[2,256]{1,0:T(2,128)S(1)}, f32[2,256,1792]{2,1,0:T(8,128)}) fusion(bf16[1792,2,128]{2,0,1:T(8,128)(2,1)S(1)} %get-tuple-element.251, pred[256,1792]{1,0:T(8,128)(4,1)S(1)} %iota_compare_fusion.6, bf16[8,256,2,128]{1,3,0,2:T(8,128)(2,1)} %get-tuple-element.250, s32[]{:T(128)S(6)} %copy.63), kind=kOutput, calls=%fused_computation.132.clone.1 | convolution fusion | flops 239470336 | bytes 5638148 | tf_op jit(solution)/shard_map/while/body/eval_jaxpr/sub | solution.py:20
  82.3 4.7 %fusion.93 = (f32[2,256]{1,0:T(2,128)S(1)}, f32[2,256,1792]{2,1,0:T(8,128)}) fusion(bf16[1792,2,128]{2,0,1:T(8,128)(2,1)S(1)} %get-tuple-element.251, pred[256,1792]{1,0:T(8,128)(4,1)S(1)} %iota_compare_fusion.6, bf16[8,256,2,128]{1,3,0,2:T(8,128)(2,1)} %get-tuple-element.250, s32[]{:T(128)S(6)} %copy.63), kind=kOutput, calls=%fused_computation.132.clone.1 | convolution fusion | flops 239470336 | bytes 5638148 | tf_op jit(solution)/shard_map/while/body/eval_jaxpr/sub | solution.py:20
  90.5 4.6 %fusion.93 = (f32[2,256]{1,0:T(2,128)S(1)}, f32[2,256,1792]{2,1,0:T(8,128)}) fusion(bf16[1792,2,128]{2,0,1:T(8,128)(2,1)S(1)} %get-tuple-element.251, pred[256,1792]{1,0:T(8,128)(4,1)S(1)} %iota_compare_fusion.6, bf16[8,256,2,128]{1,3,0,2:T(8,128)(2,1)} %get-tuple-element.250, s32[]{:T(128)S(6)} %copy.63), kind=kOutput, calls=%fused_computation.132.clone.1 | convolution fusion | flops 239470336 | bytes 5638148 | tf_op jit(solution)/shard_map/while/body/eval_jaxpr/sub | solution.py:20
  98.6 4.6 %fusion.93 = (f32[2,256]{1,0:T(2,128)S(1)}, f32[2,256,1792]{2,1,0:T(8,128)}) fusion(bf16[1792,2,128]{2,0,1:T(8,128)(2,1)S(1)} %get-tuple-element.251, pred[256,1792]{1,0:T(8,128)(4,1)S(1)} %iota_compare_fusion.6, bf16[8,256,2,128]{1,3,0,2:T(8,128)(2,1)} %get-tuple-element.250, s32[]{:T(128)S(6)} %copy.63), kind=kOutput, calls=%fused_computation.132.clone.1 | convolution fusion | flops 239470336 | bytes 5638148 | tf_op jit(solution)/shard_map/while/body/eval_jaxpr/sub | solution.py:20
  107.2 4.6 %fusion.93 = (f32[2,256]{1,0:T(2,128)S(1)}, f32[2,256,1792]{2,1,0:T(8,128)}) fusion(bf16[1792,2,128]{2,0,1:T(8,128)(2,1)S(1)} %get-tuple-element.251, pred[256,1792]{1,0:T(8,128)(4,1)S(1)} %iota_compare_fusion.6, bf16[8,256,2,128]{1,3,0,2:T(8,128)(2,1)} %get-tuple-element.250, s32[]{:T(128)S(6)} %copy.63), kind=kOutput, calls=%fused_computation.132.clone.1 | convolution fusion | flops 239470336 | bytes 5638148 | tf_op jit(solution)/shard_map/while/body/eval_jaxpr/sub | solution.py:20
  115.1 65.1 %while.20 = (s32[]{:T(128)}, bf16[8,256,2,128]{1,3,0,2:T(8,128)(2,1)S(1)}, s32[1,256]{1,0:T(1,128)S(1)}, bf16[8,256,2,128]{1,3,0,2:T(8,128)(2,1)}, bf16[1792,2,1...) while((s32[]{:T(128)}, bf16[8,256,2,128]{1,3,0,2:T(8,128)(2,1)S(1)}, ...), condition=%wide.region_9.10_spmd, body=%wide.region_6.9_spmd.sunk | while | flops 476710656 | bytes 11342941 | solution.py:123
  115.5 4.6 %fusion.88 = (f32[2,256]{1,0:T(2,128)S(1)}, f32[2,256,1792]{2,1,0:T(8,128)}) fusion(bf16[1792,2,128]{2,0,1:T(8,128)(2,1)S(1)} %get-tuple-element.272, pred[256,1792]{1,0:T(8,128)(4,1)S(1)} %iota_compare_fusion.5, bf16[8,256,2,128]{1,3,0,2:T(8,128)(2,1)} %get-tuple-element.271, s32[]{:T(128)S(6)} %copy.69), kind=kOutput, calls=%fused_computation.131.clone.1 | convolution fusion | flops 239470336 | bytes 5638148 | tf_op jit(solution)/shard_map/while/body/eval_jaxpr/sub | solution.py:20
  123.6 4.6 %fusion.88 = (f32[2,256]{1,0:T(2,128)S(1)}, f32[2,256,1792]{2,1,0:T(8,128)}) fusion(bf16[1792,2,128]{2,0,1:T(8,128)(2,1)S(1)} %get-tuple-element.272, pred[256,1792]{1,0:T(8,128)(4,1)S(1)} %iota_compare_fusion.5, bf16[8,256,2,128]{1,3,0,2:T(8,128)(2,1)} %get-tuple-element.271, s32[]{:T(128)S(6)} %copy.69), kind=kOutput, calls=%fused_computation.131.clone.1 | convolution fusion | flops 239470336 | bytes 5638148 | tf_op jit(solution)/shard_map/while/body/eval_jaxpr/sub | solution.py:20
  131.7 4.6 %fusion.88 = (f32[2,256]{1,0:T(2,128)S(1)}, f32[2,256,1792]{2,1,0:T(8,128)}) fusion(bf16[1792,2,128]{2,0,1:T(8,128)(2,1)S(1)} %get-tuple-element.272, pred[256,1792]{1,0:T(8,128)(4,1)S(1)} %iota_compare_fusion.5, bf16[8,256,2,128]{1,3,0,2:T(8,128)(2,1)} %get-tuple-element.271, s32[]{:T(128)S(6)} %copy.69), kind=kOutput, calls=%fused_computation.131.clone.1 | convolution fusion | flops 239470336 | bytes 5638148 | tf_op jit(solution)/shard_map/while/body/eval_jaxpr/sub | solution.py:20
  140.0 4.6 %fusion.88 = (f32[2,256]{1,0:T(2,128)S(1)}, f32[2,256,1792]{2,1,0:T(8,128)}) fusion(bf16[1792,2,128]{2,0,1:T(8,128)(2,1)S(1)} %get-tuple-element.272, pred[256,1792]{1,0:T(8,128)(4,1)S(1)} %iota_compare_fusion.5, bf16[8,256,2,128]{1,3,0,2:T(8,128)(2,1)} %get-tuple-element.271, s32[]{:T(128)S(6)} %copy.69), kind=kOutput, calls=%fused_computation.131.clone.1 | convolution fusion | flops 239470336 | bytes 5638148 | tf_op jit(solution)/shard_map/while/body/eval_jaxpr/sub | solution.py:20
  148.1 4.6 %fusion.88 = (f32[2,256]{1,0:T(2,128)S(1)}, f32[2,256,1792]{2,1,0:T(8,128)}) fusion(bf16[1792,2,128]{2,0,1:T(8,128)(2,1)S(1)} %get-tuple-element.272, pred[256,1792]{1,0:T(8,128)(4,1)S(1)} %iota_compare_fusion.5, bf16[8,256,2,128]{1,3,0,2:T(8,128)(2,1)} %get-tuple-element.271, s32[]{:T(128)S(6)} %copy.69), kind=kOutput, calls=%fused_computation.131.clone.1 | convolution fusion | flops 239470336 | bytes 5638148 | tf_op jit(solution)/shard_map/while/body/eval_jaxpr/sub | solution.py:20
  156.2 4.6 %fusion.88 = (f32[2,256]{1,0:T(2,128)S(1)}, f32[2,256,1792]{2,1,0:T(8,128)}) fusion(bf16[1792,2,128]{2,0,1:T(8,128)(2,1)S(1)} %get-tuple-element.272, pred[256,1792]{1,0:T(8,128)(4,1)S(1)} %iota_compare_fusion.5, bf16[8,256,2,128]{1,3,0,2:T(8,128)(2,1)} %get-tuple-element.271, s32[]{:T(128)S(6)} %copy.69), kind=kOutput, calls=%fused_computation.131.clone.1 | convolution fusion | flops 239470336 | bytes 5638148 | tf_op jit(solution)/shard_map/while/body/eval_jaxpr/sub | solution.py:20
  164.3 4.6 %fusion.88 = (f32[2,256]{1,0:T(2,128)S(1)}, f32[2,256,1792]{2,1,0:T(8,128)}) fusion(bf16[1792,2,128]{2,0,1:T(8,128)(2,1)S(1)} %get-tuple-element.272, pred[256,1792]{1,0:T(8,128)(4,1)S(1)} %iota_compare_fusion.5, bf16[8,256,2,128]{1,3,0,2:T(8,128)(2,1)} %get-tuple-element.271, s32[]{:T(128)S(6)} %copy.69), kind=kOutput, calls=%fused_computation.131.clone.1 | convolution fusion | flops 239470336 | bytes 5638148 | tf_op jit(solution)/shard_map/while/body/eval_jaxpr/sub | solution.py:20
  180.2 25.9 %convolution_convert_fusion = bf16[512,8192]{1,0:T(8,128)(2,1)} fusion(bf16[2048,8192]{1,0:T(8,128)(2,1)} %all-gather.2.cloned.1.call-done, bf16[256,2048]{0,1:T(8,128)(2,1)S(1)} %bitcast.138, bf16[256,2048]{0,1:T(8,128)(2,1)S(1)} %bitcast.139), kind=kOutput, calls=%fused_computation.48 | convolution fusion | flops 17188257792 | bytes 44040192 | tf_op jit(solution)/shard_map/dot_general | solution.py:57
  209.1 9.2 %all-reduce.2 = (s32[16]{0:T(128)S(1)}, s32[8]{0:T(128)S(1)}) all-reduce(s32[16]{0:T(128)S(1)} %dynamic-update-slice, s32[8]{0:T(128)S(1)} %dynamic-update-slice.1), channel_id=1, replica_groups=mesh['req'=8,'head'=4] {'req'}, use_global_device_ids=true, to_apply=%add | all-reduce | flops 24 | bytes 192
  224.9 128.4 %reduce-scatter.2.cloned.1.call-done = bf16[512,2048]{1,0:T(8,128)(2,1)} async-done(((bf16[512,8192]{1,0:T(8,128)(2,1)}), bf16[512,2048]{1,0:T(8,128)(2,1)}) %reduce-scatter.2.cloned.1.call-update) | async-done | bytes 2097168 | tf_op jit(solution)/shard_map/reduce_scatter | solution.py:65
  353.4 6.3 %gather_fusion.5 = bf16[512,2048]{1,0:T(8,128)(2,1)S(1)} fusion(bf16[512,2048]{1,0:T(8,128)(2,1)} %reduce-scatter.2.cloned.1.call-done, s32[1024]{0:T(1024)S(1)} %pad_clamp_fusion), kind=kCustom, calls=%fused_computation.5 | custom fusion | bytes 4196352 | tf_op jit(solution)/shard_map/jit(_take)/gather | solution.py:45
  365.4 26.2 %all-to-all-done = bf16[8,64,2048]{2,1,0:T(8,128)(2,1)S(1)} async-done(((bf16[8,64,2048]{2,1,0:T(8,128)(2,1)}), bf16[8,64,2048]{2,1,0:T(8,128)(2,1)S(1)}, u32[]{:S(2)}, u32[]{:S(2)}) %all-to-all-start) | async-done | bytes 2097184 | tf_op jit(solution)/shard_map/all_to_all | solution.py:47
  (163 shorter events, 112.7 us)
Async XLA Ops:
  7.2 173.0 %all-gather.2.cloned.1.call-start = ((), (), s32[]{:S(2)}) async-start(), calls=%async_computation.2 | async-start | bytes 37748736 | tf_op jit(solution)/shard_map/all_gather | solution.py:59
  10.1 0.7 copy-start.9
  10.1 0.9 copy-start.10
  10.1 0.9 copy-start
  10.2 5.7 %copy-start.7 = (bf16[512,256]{1,0:T(8,128)(2,1)S(1)}, bf16[512,256]{1,0:T(8,128)(2,1)}, u32[]{:S(2)}) copy-start(bf16[512,256]{1,0:T(8,128)(2,1)} %param.16) | copy-start | bytes 786436
  10.2 343.2 %reduce-scatter.2.cloned.1.call-start = ((), (), s32[]{:S(2)}) async-start(), calls=%async_computation.3 | async-start | bytes 10485760 | tf_op jit(solution)/shard_map/reduce_scatter | solution.py:65
  15.9 9.1 %copy-start.2 = (bf16[28,128,256]{2,1,0:T(8,128)(2,1)S(1)}, bf16[28,128,256]{2,1,0:T(8,128)(2,1)}, u32[]{:S(2)}) copy-start(bf16[28,128,256]{2,1,0:T(8,128)(2,1)} %param.19) | copy-start | bytes 5505028
  15.9 9.1 %copy-start.8 = (bf16[512,256]{1,0:T(8,128)(2,1)S(1)}, bf16[512,256]{1,0:T(8,128)(2,1)}, u32[]{:S(2)}) copy-start(bf16[512,256]{1,0:T(8,128)(2,1)} %param.17) | copy-start | bytes 786436
  28.5 6.2 %copy-start.1 = (bf16[3584,256]{1,0:T(8,128)(2,1)}, bf16[3584,256]{1,0:T(8,128)(2,1)S(1)}, u32[]{:S(2)}) copy-start(bf16[3584,256]{1,0:T(8,128)(2,1)S(1)} %scatter_fusion.1) | copy-start | bytes 5505028
  37.4 2.4 copy-start.4
  40.0 1.5 copy-start.5
  44.1 2.4 copy-start.3
  46.7 1.5 copy-start.6
  206.1 0.7 copy-start.11
  361.4 30.3 %all-to-all-start = ((bf16[8,64,2048]{2,1,0:T(8,128)(2,1)}), bf16[8,64,2048]{2,1,0:T(8,128)(2,1)S(1)}, u32[]{:S(2)}, u32[]{:S(2)}) async-start(bf16[8,64,2048]{2,1,0:T(8,128)(2,1)} %select_select_fusion), calls=%async_computation.1 | async-start | bytes 4194304 | tf_op jit(solution)/shard_map/all_to_all | solution.py:47
Sparse Core Ops, SparseCore 0:
  10.3 163.3 all-gather.1
  206.3 147.0 reduce-scatter.1
where the time goes:
time: 406 us; the launch traced here: 405 us
  waiting for transfers between devices  155 us (38%)
  matrix products  150 us (37%)
  local copies, waits for them, and re-layouts  59.2 us (15%)
  between operations  15.6 us (4%)
  other arithmetic  11.8 us (3%)
  blocking collectives  9.17 us (2%)
    reduce_scatter x1, waiting for transfers between devices, head_total(): lax.psum_scatter(partial_sum.astype(jnp.bfloat16), 'head', scatter_dimens...  128 us
    sub x16, matrix products, head_attention(): expo_terms = jnp.where(allowed, jnp.exp(scores - highest), 0.0)  74.1 us
    dot_general x16, matrix products, head_attention(): jnp.einsum('kts,skd->tkd', weights, prior_values, preferred_element_type=...  49.8 us
    all_to_all x1, waiting for transfers between devices, deal(): lax.all_to_all(outgoing, 'req', split_axis=0, concat_axis=0, tiled=True)  26.2 us
    dot_general x1, matrix products, project(): jnp.dot(row_block, lax.all_gather(out_weight, 'req', axis=1, tiled=True),...  25.9 us
    unnamed x40, local copies, waits for them, and re-layouts  9.63 us
    unnamed x1, blocking collectives  9.17 us
  transfers between devices with their start and end apart: 3, of which 2 were waited for; matrix products, arithmetic and copies ran while one was open for 44% of the time, Pallas kernels for 0%

commit v1 on v0

--- a/solution.py
+++ b/solution.py
@@ -1,3 +1,4 @@
+import functools
 import math
 import jax
 import jax.numpy as jnp
@@ -6,6 +7,29 @@
 
 HEAD_SIZE = 128
 NEGATIVE = -1e30
+
+
+def recover_leaves(m, named_axis):
+    front = jax.lax.psum(1, named_axis)
+    seen_now = jax.lax.axis_index(named_axis)
+    val2, plain = (front, seen_now)
+    res = m.shape[0] // val2
+    field_out = list(m.shape)
+    field_out[0] = res
+    later = field_out[0]
+    field_out[0] = later * val2
+    f_now = jnp.zeros(field_out, m.dtype)
+    for to_i in range(val2):
+        k_now = lax.dynamic_slice_in_dim(m, (plain ^ to_i) * res, res, axis=0)
+        if to_i:
+            k_now = jax.lax.ppermute(
+                k_now, named_axis, list(map(lambda rr: (rr, rr ^ to_i), range(val2)))
+            )
+        f_now = lax.dynamic_update_slice_in_dim(f_now, k_now, (plain ^ to_i) * later, axis=0)
+    return f_now
+
+
+shards_load = functools.partial(recover_leaves, named_axis="req")
 
 
 def head_attention(query_matrix, prior_keys, prior_values, visible, scale_factor):
@@ -44,7 +68,7 @@
     source = jnp.where(is_live, source, 0)
     picked = jnp.take(row_block, source.reshape(-1), axis=0).reshape(groups, pair_slots, columns)
     outgoing = jnp.where(is_live[:, :, None], picked, jnp.zeros((), row_block.dtype))
-    arrived = lax.all_to_all(outgoing, "req", split_axis=0, concat_axis=0, tiled=True)
+    arrived = shards_load(outgoing)
     own_shares = lax.dynamic_index_in_dim(shares, my_rank, 1, keepdims=False)
     own_starts = lax.dynamic_index_in_dim(starts, my_rank, 1, keepdims=False)
     within = jnp.arange(pair_slots, dtype=jnp.int32)[None, :]

time: 406 us -> 417 us (1.027)
  waiting for transfers between devices: 155 us -> 162 us
    all_to_all x1 -> x0, waiting for transfers between devices: 26.2 us -> none  [deal(): lax.all_to_all(outgoing, 'req', split_axis=0, concat_axis=0, tiled=True)]
    ppermute x0 -> x7, waiting for transfers between devices: none -> 18.1 us  [recover_leaves(): jax.lax.ppermute(k_now, named_axis, list(map(lambda rr: (rr, rr ^ to_i),...]
    reduce_scatter x1, waiting for transfers between devices: 128 us -> 143 us  [head_total(): lax.psum_scatter(partial_sum.astype(jnp.bfloat16), 'head', scatter_dimens...]
    ppermute x0 -> x7, starting transfers between devices: none -> 7.06 us  [recover_leaves(): jax.lax.ppermute(k_now, named_axis, list(map(lambda rr: (rr, rr ^ to_i),...]
  transfers between devices with their start and end apart: 3 -> 9, of which waited for: 2 -> 5; matrix products, arithmetic and copies ran while one was open for 44% -> 43% of each run, Pallas kernels for 0% -> 0%
where the time goes in v1:
time: 417 us; the launch traced here: 415 us
  waiting for transfers between devices  162 us (39%)
  matrix products  150 us (36%)
  local copies, waits for them, and re-layouts  60.7 us (15%)
  between operations  15.8 us (4%)
  other arithmetic  10.2 us (2%)
  blocking collectives  9.49 us (2%)
  starting transfers between devices  7.13 us (2%)
    reduce_scatter x1, waiting for transfers between devices, head_total(): lax.psum_scatter(partial_sum.astype(jnp.bfloat16), 'head', scatter_dimens...  143 us
    sub x16, matrix products, head_attention(): expo_terms = jnp.where(allowed, jnp.exp(scores - highest), 0.0)  74.2 us
    dot_general x16, matrix products, head_attention(): jnp.einsum('kts,skd->tkd', weights, prior_values, preferred_element_type=...  49.7 us
    dot_general x1, matrix products, project(): jnp.dot(row_block, lax.all_gather(out_weight, 'req', axis=1, tiled=True),...  25.9 us
    ppermute x7, waiting for transfers between devices, recover_leaves(): jax.lax.ppermute(k_now, named_axis, list(map(lambda rr: (rr, rr ^ to_i),...  18.1 us
    unnamed x1, blocking collectives  9.49 us
    unnamed x40, local copies, waits for them, and re-layouts  9.07 us
  transfers between devices with their start and end apart: 9, of which 5 were waited for; matrix products, arithmetic and copies ran while one was open for 43% of the time, Pallas kernels for 0%

profile of v1, /device:TPU:0, one launch (start us, length us, event | category | flops | bytes accessed | tf_op | source)
XLA Modules:
  0.0 415.4 jit_solution(9510954244406747797)
XLA Ops:
  13.1 9.5 %all-reduce.2 = (s32[16]{0:T(128)S(1)}, s32[8]{0:T(128)S(1)}) all-reduce(s32[16]{0:T(128)S(1)} %dynamic-update-slice, s32[8]{0:T(128)S(1)} %dynamic-update-slice.1), channel_id=1, replica_groups=mesh['req'=8,'head'=4] {'req'}, use_global_device_ids=true, to_apply=%add | all-reduce | flops 24 | bytes 192
  27.9 4.8 %gather_fusion.6 = s32[512]{0:T(512)S(1)} fusion(s32[2,14]{1,0:T(2,128)S(1)} %copy-done, s32[512]{0:T(512)S(1)} %bitcast.125), kind=kCustom, calls=%fused_computation.6 | custom fusion | bytes 8192 | tf_op jit(solution)/shard_map/jit(take_along_axis)/gather | solution.py:120
  33.3 5.5 %scatter_fusion = bf16[3584,256]{1,0:T(8,128)(2,1)} fusion(bf16[3584,256]{1,0:T(8,128)(2,1)} %bitcast.130, s32[512]{0:T(512)S(1)} %bitcast.143, bf16[512,256]{1,0:T(8,128)(2,1)S(1)} %copy-done.7), kind=kCustom, calls=%fused_computation.7 | custom fusion | bytes 788480 | tf_op jit(solution)/shard_map/scatter | solution.py:127
  65.1 66.5 %while.21 = (s32[]{:T(128)}, bf16[8,256,2,128]{1,3,0,2:T(8,128)(2,1)S(1)}, s32[1,256]{1,0:T(1,128)S(1)}, bf16[8,256,2,128]{1,3,0,2:T(8,128)(2,1)}, bf16[1792,2,1...) while((s32[]{:T(128)}, bf16[8,256,2,128]{1,3,0,2:T(8,128)(2,1)S(1)}, ...), condition=%wide.region_13.14_spmd, body=%wide.region_10.13_spmd.sunk | while | flops 476710656 | bytes 11342941 | solution.py:147
  65.4 4.6 %fusion.95 = (f32[2,256]{1,0:T(2,128)S(1)}, f32[2,256,1792]{2,1,0:T(8,128)}) fusion(bf16[1792,2,128]{2,0,1:T(8,128)(2,1)S(1)} %get-tuple-element.259, pred[256,1792]{1,0:T(8,128)(4,1)S(1)} %iota_compare_fusion.6, bf16[8,256,2,128]{1,3,0,2:T(8,128)(2,1)} %get-tuple-element.258, s32[]{:T(128)S(6)} %copy.63), kind=kOutput, calls=%fused_computation.149.clone.1 | convolution fusion | flops 239470336 | bytes 5638148 | tf_op jit(solution)/shard_map/while/body/eval_jaxpr/sub | solution.py:44
  73.5 4.6 %fusion.95 = (f32[2,256]{1,0:T(2,128)S(1)}, f32[2,256,1792]{2,1,0:T(8,128)}) fusion(bf16[1792,2,128]{2,0,1:T(8,128)(2,1)S(1)} %get-tuple-element.259, pred[256,1792]{1,0:T(8,128)(4,1)S(1)} %iota_compare_fusion.6, bf16[8,256,2,128]{1,3,0,2:T(8,128)(2,1)} %get-tuple-element.258, s32[]{:T(128)S(6)} %copy.63), kind=kOutput, calls=%fused_computation.149.clone.1 | convolution fusion | flops 239470336 | bytes 5638148 | tf_op jit(solution)/shard_map/while/body/eval_jaxpr/sub | solution.py:44
  83.0 4.7 %fusion.95 = (f32[2,256]{1,0:T(2,128)S(1)}, f32[2,256,1792]{2,1,0:T(8,128)}) fusion(bf16[1792,2,128]{2,0,1:T(8,128)(2,1)S(1)} %get-tuple-element.259, pred[256,1792]{1,0:T(8,128)(4,1)S(1)} %iota_compare_fusion.6, bf16[8,256,2,128]{1,3,0,2:T(8,128)(2,1)} %get-tuple-element.258, s32[]{:T(128)S(6)} %copy.63), kind=kOutput, calls=%fused_computation.149.clone.1 | convolution fusion | flops 239470336 | bytes 5638148 | tf_op jit(solution)/shard_map/while/body/eval_jaxpr/sub | solution.py:44
  91.2 4.6 %fusion.95 = (f32[2,256]{1,0:T(2,128)S(1)}, f32[2,256,1792]{2,1,0:T(8,128)}) fusion(bf16[1792,2,128]{2,0,1:T(8,128)(2,1)S(1)} %get-tuple-element.259, pred[256,1792]{1,0:T(8,128)(4,1)S(1)} %iota_compare_fusion.6, bf16[8,256,2,128]{1,3,0,2:T(8,128)(2,1)} %get-tuple-element.258, s32[]{:T(128)S(6)} %copy.63), kind=kOutput, calls=%fused_computation.149.clone.1 | convolution fusion | flops 239470336 | bytes 5638148 | tf_op jit(solution)/shard_map/while/body/eval_jaxpr/sub | solution.py:44
  99.3 4.6 %fusion.95 = (f32[2,256]{1,0:T(2,128)S(1)}, f32[2,256,1792]{2,1,0:T(8,128)}) fusion(bf16[1792,2,128]{2,0,1:T(8,128)(2,1)S(1)} %get-tuple-element.259, pred[256,1792]{1,0:T(8,128)(4,1)S(1)} %iota_compare_fusion.6, bf16[8,256,2,128]{1,3,0,2:T(8,128)(2,1)} %get-tuple-element.258, s32[]{:T(128)S(6)} %copy.63), kind=kOutput, calls=%fused_computation.149.clone.1 | convolution fusion | flops 239470336 | bytes 5638148 | tf_op jit(solution)/shard_map/while/body/eval_jaxpr/sub | solution.py:44
  107.5 4.6 %fusion.95 = (f32[2,256]{1,0:T(2,128)S(1)}, f32[2,256,1792]{2,1,0:T(8,128)}) fusion(bf16[1792,2,128]{2,0,1:T(8,128)(2,1)S(1)} %get-tuple-element.259, pred[256,1792]{1,0:T(8,128)(4,1)S(1)} %iota_compare_fusion.6, bf16[8,256,2,128]{1,3,0,2:T(8,128)(2,1)} %get-tuple-element.258, s32[]{:T(128)S(6)} %copy.63), kind=kOutput, calls=%fused_computation.149.clone.1 | convolution fusion | flops 239470336 | bytes 5638148 | tf_op jit(solution)/shard_map/while/body/eval_jaxpr/sub | solution.py:44
  115.6 4.6 %fusion.95 = (f32[2,256]{1,0:T(2,128)S(1)}, f32[2,256,1792]{2,1,0:T(8,128)}) fusion(bf16[1792,2,128]{2,0,1:T(8,128)(2,1)S(1)} %get-tuple-element.259, pred[256,1792]{1,0:T(8,128)(4,1)S(1)} %iota_compare_fusion.6, bf16[8,256,2,128]{1,3,0,2:T(8,128)(2,1)} %get-tuple-element.258, s32[]{:T(128)S(6)} %copy.63), kind=kOutput, calls=%fused_computation.149.clone.1 | convolution fusion | flops 239470336 | bytes 5638148 | tf_op jit(solution)/shard_map/while/body/eval_jaxpr/sub | solution.py:44
  123.8 4.6 %fusion.95 = (f32[2,256]{1,0:T(2,128)S(1)}, f32[2,256,1792]{2,1,0:T(8,128)}) fusion(bf16[1792,2,128]{2,0,1:T(8,128)(2,1)S(1)} %get-tuple-element.259, pred[256,1792]{1,0:T(8,128)(4,1)S(1)} %iota_compare_fusion.6, bf16[8,256,2,128]{1,3,0,2:T(8,128)(2,1)} %get-tuple-element.258, s32[]{:T(128)S(6)} %copy.63), kind=kOutput, calls=%fused_computation.149.clone.1 | convolution fusion | flops 239470336 | bytes 5638148 | tf_op jit(solution)/shard_map/while/body/eval_jaxpr/sub | solution.py:44
  131.6 65.3 %while.20 = (s32[]{:T(128)}, bf16[8,256,2,128]{1,3,0,2:T(8,128)(2,1)S(1)}, s32[1,256]{1,0:T(1,128)S(1)}, bf16[8,256,2,128]{1,3,0,2:T(8,128)(2,1)}, bf16[1792,2,1...) while((s32[]{:T(128)}, bf16[8,256,2,128]{1,3,0,2:T(8,128)(2,1)S(1)}, ...), condition=%wide.region_9.10_spmd, body=%wide.region_6.9_spmd.sunk | while | flops 476710656 | bytes 11342941 | solution.py:147
  132.0 4.6 %fusion.90 = (f32[2,256]{1,0:T(2,128)S(1)}, f32[2,256,1792]{2,1,0:T(8,128)}) fusion(bf16[1792,2,128]{2,0,1:T(8,128)(2,1)S(1)} %get-tuple-element.280, pred[256,1792]{1,0:T(8,128)(4,1)S(1)} %iota_compare_fusion.5, bf16[8,256,2,128]{1,3,0,2:T(8,128)(2,1)} %get-tuple-element.279, s32[]{:T(128)S(6)} %copy.69), kind=kOutput, calls=%fused_computation.148.clone.1 | convolution fusion | flops 239470336 | bytes 5638148 | tf_op jit(solution)/shard_map/while/body/eval_jaxpr/sub | solution.py:44
  140.3 4.6 %fusion.90 = (f32[2,256]{1,0:T(2,128)S(1)}, f32[2,256,1792]{2,1,0:T(8,128)}) fusion(bf16[1792,2,128]{2,0,1:T(8,128)(2,1)S(1)} %get-tuple-element.280, pred[256,1792]{1,0:T(8,128)(4,1)S(1)} %iota_compare_fusion.5, bf16[8,256,2,128]{1,3,0,2:T(8,128)(2,1)} %get-tuple-element.279, s32[]{:T(128)S(6)} %copy.69), kind=kOutput, calls=%fused_computation.148.clone.1 | convolution fusion | flops 239470336 | bytes 5638148 | tf_op jit(solution)/shard_map/while/body/eval_jaxpr/sub | solution.py:44
  148.4 4.7 %fusion.90 = (f32[2,256]{1,0:T(2,128)S(1)}, f32[2,256,1792]{2,1,0:T(8,128)}) fusion(bf16[1792,2,128]{2,0,1:T(8,128)(2,1)S(1)} %get-tuple-element.280, pred[256,1792]{1,0:T(8,128)(4,1)S(1)} %iota_compare_fusion.5, bf16[8,256,2,128]{1,3,0,2:T(8,128)(2,1)} %get-tuple-element.279, s32[]{:T(128)S(6)} %copy.69), kind=kOutput, calls=%fused_computation.148.clone.1 | convolution fusion | flops 239470336 | bytes 5638148 | tf_op jit(solution)/shard_map/while/body/eval_jaxpr/sub | solution.py:44
  156.6 4.6 %fusion.90 = (f32[2,256]{1,0:T(2,128)S(1)}, f32[2,256,1792]{2,1,0:T(8,128)}) fusion(bf16[1792,2,128]{2,0,1:T(8,128)(2,1)S(1)} %get-tuple-element.280, pred[256,1792]{1,0:T(8,128)(4,1)S(1)} %iota_compare_fusion.5, bf16[8,256,2,128]{1,3,0,2:T(8,128)(2,1)} %get-tuple-element.279, s32[]{:T(128)S(6)} %copy.69), kind=kOutput, calls=%fused_computation.148.clone.1 | convolution fusion | flops 239470336 | bytes 5638148 | tf_op jit(solution)/shard_map/while/body/eval_jaxpr/sub | solution.py:44
  164.7 4.6 %fusion.90 = (f32[2,256]{1,0:T(2,128)S(1)}, f32[2,256,1792]{2,1,0:T(8,128)}) fusion(bf16[1792,2,128]{2,0,1:T(8,128)(2,1)S(1)} %get-tuple-element.280, pred[256,1792]{1,0:T(8,128)(4,1)S(1)} %iota_compare_fusion.5, bf16[8,256,2,128]{1,3,0,2:T(8,128)(2,1)} %get-tuple-element.279, s32[]{:T(128)S(6)} %copy.69), kind=kOutput, calls=%fused_computation.148.clone.1 | convolution fusion | flops 239470336 | bytes 5638148 | tf_op jit(solution)/shard_map/while/body/eval_jaxpr/sub | solution.py:44
  181.1 4.6 %fusion.90 = (f32[2,256]{1,0:T(2,128)S(1)}, f32[2,256,1792]{2,1,0:T(8,128)}) fusion(bf16[1792,2,128]{2,0,1:T(8,128)(2,1)S(1)} %get-tuple-element.280, pred[256,1792]{1,0:T(8,128)(4,1)S(1)} %iota_compare_fusion.5, bf16[8,256,2,128]{1,3,0,2:T(8,128)(2,1)} %get-tuple-element.279, s32[]{:T(128)S(6)} %copy.69), kind=kOutput, calls=%fused_computation.148.clone.1 | convolution fusion | flops 239470336 | bytes 5638148 | tf_op jit(solution)/shard_map/while/body/eval_jaxpr/sub | solution.py:44
  189.2 4.6 %fusion.90 = (f32[2,256]{1,0:T(2,128)S(1)}, f32[2,256,1792]{2,1,0:T(8,128)}) fusion(bf16[1792,2,128]{2,0,1:T(8,128)(2,1)S(1)} %get-tuple-element.280, pred[256,1792]{1,0:T(8,128)(4,1)S(1)} %iota_compare_fusion.5, bf16[8,256,2,128]{1,3,0,2:T(8,128)(2,1)} %get-tuple-element.279, s32[]{:T(128)S(6)} %copy.69), kind=kOutput, calls=%fused_computation.148.clone.1 | convolution fusion | flops 239470336 | bytes 5638148 | tf_op jit(solution)/shard_map/while/body/eval_jaxpr/sub | solution.py:44
  197.0 25.9 %convolution_convert_fusion = bf16[512,8192]{1,0:T(8,128)(2,1)} fusion(bf16[2048,8192]{1,0:T(8,128)(2,1)} %all-gather.2.cloned.1.call-done, bf16[256,2048]{0,1:T(8,128)(2,1)S(1)} %bitcast.138, bf16[256,2048]{0,1:T(8,128)(2,1)S(1)} %bitcast.139), kind=kOutput, calls=%fused_computation.48 | convolution fusion | flops 17188257792 | bytes 44040192 | tf_op jit(solution)/shard_map/dot_general | solution.py:81
  224.1 143.4 %reduce-scatter.2.cloned.1.call-done = bf16[512,2048]{1,0:T(8,128)(2,1)} async-done(((bf16[512,8192]{1,0:T(8,128)(2,1)}), bf16[512,2048]{1,0:T(8,128)(2,1)}) %reduce-scatter.2.cloned.1.call-update) | async-done | bytes 2097168 | tf_op jit(solution)/shard_map/reduce_scatter | solution.py:89
  367.5 6.5 %gather_fusion.5 = bf16[512,2048]{1,0:T(8,128)(2,1)S(1)} fusion(bf16[512,2048]{1,0:T(8,128)(2,1)} %reduce-scatter.2.cloned.1.call-done, s32[1024]{0:T(1024)S(1)} %pad_clamp_fusion), kind=kCustom, calls=%fused_computation.5 | custom fusion | bytes 4196352 | tf_op jit(solution)/shard_map/jit(_take)/gather | solution.py:69
  389.9 12.1 %collective-permute-done.4 = bf16[1,64,2048]{2,1,0:T(8,128)(2,1)S(1)} collective-permute-done((bf16[1,64,2048]{2,1,0:T(8,128)(2,1)S(1)}, bf16[1,64,2048]{2,1,0:T(8,128)(2,1)S(1)}, u32[]{:S(2)}, u32[]{:S(2)}) %collective-permute-start.4) | collective-permute-done | bytes 262176 | tf_op jit(solution)/shard_map/ppermute | solution.py:25
  (184 shorter events, 121.7 us)
Async XLA Ops:
  7.2 189.8 %all-gather.2.cloned.1.call-start = ((), (), s32[]{:S(2)}) async-start(), calls=%async_computation.1 | async-start | bytes 37748736 | tf_op jit(solution)/shard_map/all_gather | solution.py:83
  10.1 0.7 copy-start.11
  10.1 2.0 copy-start.10
  10.1 14.0 %copy-start.9 = (s32[2]{0:T(128)S(1)}, s32[2]{0:T(128)}, u32[]{:S(2)}) copy-start(s32[2]{0:T(128)} %param.22) | copy-start | bytes 28
  10.2 357.3 %reduce-scatter.2.cloned.1.call-start = ((), (), s32[]{:S(2)}) async-start(), calls=%async_computation.2 | async-start | bytes 10485760 | tf_op jit(solution)/shard_map/reduce_scatter | solution.py:89
  24.5 3.4 copy-start
  27.9 5.4 %copy-start.7 = (bf16[512,256]{1,0:T(8,128)(2,1)S(1)}, bf16[512,256]{1,0:T(8,128)(2,1)}, u32[]{:S(2)}) copy-start(bf16[512,256]{1,0:T(8,128)(2,1)} %param.16) | copy-start | bytes 786436
  33.2 8.6 %copy-start.2 = (bf16[28,128,256]{2,1,0:T(8,128)(2,1)S(1)}, bf16[28,128,256]{2,1,0:T(8,128)(2,1)}, u32[]{:S(2)}) copy-start(bf16[28,128,256]{2,1,0:T(8,128)(2,1)} %param.19) | copy-start | bytes 5505028
  33.3 8.6 %copy-start.8 = (bf16[512,256]{1,0:T(8,128)(2,1)S(1)}, bf16[512,256]{1,0:T(8,128)(2,1)}, u32[]{:S(2)}) copy-start(bf16[512,256]{1,0:T(8,128)(2,1)} %param.17) | copy-start | bytes 786436
  45.4 6.2 %copy-start.1 = (bf16[3584,256]{1,0:T(8,128)(2,1)}, bf16[3584,256]{1,0:T(8,128)(2,1)S(1)}, u32[]{:S(2)}) copy-start(bf16[3584,256]{1,0:T(8,128)(2,1)S(1)} %scatter_fusion.1) | copy-start | bytes 5505028
  54.3 2.4 copy-start.4
  56.9 1.5 copy-start.5
  60.9 2.4 copy-start.3
  63.6 1.5 copy-start.6
  375.6 3.7 collective-permute-start
  375.8 9.4 %collective-permute-start.1 = (bf16[1,64,2048]{2,1,0:T(8,128)(2,1)}, bf16[1,64,2048]{2,1,0:T(8,128)(2,1)S(1)}, u32[]{:S(2)}, u32[]{:S(2)}) collective-permute-start(bf16[1,64,2048]{2,1,0:T(8,128)(2,1)} %get-tuple-element.140), channel_id=1, source_target_pairs={{0,8},{4,12},{8,0},{12,4},{16,24},{20,28},{24,16},{28,20},{1,9},{5... | collective-permute-start | bytes 786440 | tf_op jit(solution)/shard_map/ppermute | solution.py:25
  377.3 12.6 %collective-permute-start.2 = (bf16[1,64,2048]{2,1,0:T(8,128)(2,1)S(1)}, bf16[1,64,2048]{2,1,0:T(8,128)(2,1)S(1)}, u32[]{:S(2)}, u32[]{:S(2)}) collective-permute-start(bf16[1,64,2048]{2,1,0:T(8,128)(2,1)S(1)} %get-tuple-element.139), channel_id=1, source_target_pairs={{0,12},{4,8},{8,4},{12,0},{16,28},{20,24},{24,20},{28,16},{1,13},{... | collective-permute-start | bytes 786440 | tf_op jit(solution)/shard_map/ppermute | solution.py:25
  377.6 12.2 %collective-permute-start.3 = (bf16[1,64,2048]{2,1,0:T(8,128)(2,1)S(1)}, bf16[1,64,2048]{2,1,0:T(8,128)(2,1)S(1)}, u32[]{:S(2)}, u32[]{:S(2)}) collective-permute-start(bf16[1,64,2048]{2,1,0:T(8,128)(2,1)S(1)} %get-tuple-element.138), channel_id=1, source_target_pairs={{0,16},{4,20},{8,24},{12,28},{16,0},{20,4},{24,8},{28,12},{1,17},{... | collective-permute-start | bytes 786440 | tf_op jit(solution)/shard_map/ppermute | solution.py:25
  379.1 22.9 %collective-permute-start.4 = (bf16[1,64,2048]{2,1,0:T(8,128)(2,1)S(1)}, bf16[1,64,2048]{2,1,0:T(8,128)(2,1)S(1)}, u32[]{:S(2)}, u32[]{:S(2)}) collective-permute-start(bf16[1,64,2048]{2,1,0:T(8,128)(2,1)S(1)} %get-tuple-element.137), channel_id=1, source_target_pairs={{0,20},{4,16},{8,28},{12,24},{16,4},{20,0},{24,12},{28,8},{1,21},{... | collective-permute-start | bytes 786440 | tf_op jit(solution)/shard_map/ppermute | solution.py:25
  379.3 22.7 %collective-permute-start.5 = (bf16[1,64,2048]{2,1,0:T(8,128)(2,1)S(1)}, bf16[1,64,2048]{2,1,0:T(8,128)(2,1)S(1)}, u32[]{:S(2)}, u32[]{:S(2)}) collective-permute-start(bf16[1,64,2048]{2,1,0:T(8,128)(2,1)S(1)} %get-tuple-element.136), channel_id=1, source_target_pairs={{0,24},{4,28},{8,16},{12,20},{16,8},{20,12},{24,0},{28,4},{1,25},{... | collective-permute-start | bytes 786440 | tf_op jit(solution)/shard_map/ppermute | solution.py:25
  385.2 16.9 %collective-permute-start.6 = (bf16[1,64,2048]{2,1,0:T(8,128)(2,1)S(1)}, bf16[1,64,2048]{2,1,0:T(8,128)(2,1)S(1)}, u32[]{:S(2)}, u32[]{:S(2)}) collective-permute-start(bf16[1,64,2048]{2,1,0:T(8,128)(2,1)S(1)} %get-tuple-element.135), channel_id=1, source_target_pairs={{0,28},{4,24},{8,20},{12,16},{16,12},{20,8},{24,4},{28,0},{1,29},{... | collective-permute-start | bytes 786440 | tf_op jit(solution)/shard_map/ppermute | solution.py:25
Sparse Core Ops, SparseCore 0:
  10.3 163.3 all-gather.1
  223.1 144.3 reduce-scatter.1
